TPU v7x, 128 devices: a whole 4x4x4 slice. The times are simulated.
128 devices in a mesh: dp: 32 (over y, z, x_hi), mp: 4 (over x_lo, core).
Axes of the slice: x: 4 (x_hi: 2, x_lo: 2; x = x_hi * 2 + x_lo), y: 4, z: 4, core: 2. Of those that a mesh axis runs over, the one named last changes fastest.
Arguments:
- tokens: bfloat16 [8192, 2048], P('dp'), may hold values from -6 to 6
- lengths: int32 [4], replicated, may hold values from 1 to 4096, 8192 in all
- w_query: float32 [2048, 2048], P('dp', 'mp')
- w_key: float32 [2048, 2048], P('dp', 'mp')
- w_value: float32 [2048, 2048], P('dp', 'mp'), may hold values from -0.125 to 0.125
- w_out: float32 [2048, 2048], P('dp', 'mp'), may hold values from -0.125 to 0.125
- w_gate: float32 [2048, 4096], P('dp', 'mp'), may hold values from -0.125 to 0.125
- w_up: float32 [2048, 4096], P('dp', 'mp'), may hold values from -0.125 to 0.125
- w_down: float32 [4096, 2048], P('dp', 'mp'), may hold values from -0.09375 to 0.09375
Outputs:
- layer_out: bfloat16 [8192, 2048], P(('dp', 'mp'))
Inputs may be any that keep to these rules, and one draw needn't show every extreme that they name: Every prompt is 1 to 4096 tokens long and one is exactly 4096; the lengths sum to 8192.
All inputs are finite; a program needn't handle non-finite values.
Results may differ from a plain program's by a relative error of at most 0.02.
The roundings to bfloat16 on the way count: a program that leaves them out, or rounds other values in their place, can miss the bound.
Values may be sent and summed in bfloat16 or wider, within the bound.
No kernel may reach another device: no remote copies, remote signals or barrier semaphores. Data moves between devices by JAX's collectives and lax.ppermute only.
A program may use at most 128 MiB of HBM per device.

v0:
```python
import jax
import jax.numpy as jnp
from jax import lax
from jax.sharding import PartitionSpec as P

HEAD = 128
epsilon = 1e-05
theta_base = 10000.0


def passed_along(value, axis, steps):
    count = lax.axis_size(axis)
    initial, last = (max(0, -steps), min(count, count - steps))
    return lax.ppermute(value, axis, [(source, source + steps) for source in range(initial, last)])


def layer_norm(rows):
    values = rows.astype(jnp.float32)
    centre = jnp.mean(values, axis=-1, keepdims=True)
    spread = jnp.mean(jnp.square(values - centre), axis=-1, keepdims=True)
    return (values - centre) * lax.rsqrt(spread + epsilon)


def prompt_coords(first, count, lengths):
    where = first + jnp.arange(count)
    ends = jnp.cumsum(lengths)
    passed = (ends[None, :] <= where[:, None]).astype(jnp.int32)
    prompt = jnp.sum(passed, axis=1)
    offset = where - jnp.sum(passed * lengths[None, :], axis=1)
    prompt = jnp.where(where < 0, -1, prompt)
    return (prompt, offset, where)


def rotate(values, offset):
    half = values.shape[-1] // 2
    freqs = jnp.power(theta_base, -jnp.arange(half, dtype=jnp.float32) * 2.0 / values.shape[-1])
    angles = offset.astype(jnp.float32)[:, None] * freqs[None, :]
    cosine = jnp.cos(angles)[:, None, :]
    sine = jnp.sin(angles)[:, None, :]
    first_half = values[..., :half]
    second_half = values[..., half:]
    return jnp.concatenate(
        [first_half * cosine - second_half * sine, second_half * cosine + first_half * sine],
        axis=-1,
    )


def row_product(left, pieces):
    block = jnp.concatenate(pieces, axis=1)
    return jnp.dot(left, block, preferred_element_type=jnp.float32)


def on_device(tokens, lengths, w_query, w_key, w_value, w_out, w_gate, w_up, w_down):
    half_type = jnp.bfloat16
    rows = tokens.shape[0]
    narrow = w_query.shape[1]
    heads_dev = narrow // HEAD
    dp_index = lax.axis_index("dp")
    mp_index = lax.axis_index("mp")
    reach = lax.axis_size("dp") // 2
    normed = layer_norm(tokens).astype(half_type)
    joined = row_product(
        normed,
        (
            lax.all_gather(w_query.astype(half_type), "dp", axis=0, tiled=True),
            lax.all_gather(w_key.astype(half_type), "dp", axis=0, tiled=True),
            lax.all_gather(w_value.astype(half_type), "dp", axis=0, tiled=True),
        ),
    )
    q_prompt, q_offset, q_where = prompt_coords(dp_index * rows, rows, lengths)
    shaped = joined.reshape(rows, 3, heads_dev, HEAD)
    query = rotate(shaped[:, 0], q_offset).astype(half_type)
    keys = rotate(shaped[:, 1], q_offset).astype(half_type)
    values = shaped[:, 2].astype(half_type)
    own_first = dp_index * rows
    own_pair = jnp.stack((keys, values))
    scale = 1.0 / HEAD**0.5

    def online_step(state, pair, first):
        accum, total, top = state
        k_prompt, k_offset, k_where = prompt_coords(first, rows, lengths)
        scores = (
            jnp.einsum("qhd,khd->hqk", query, pair[0], preferred_element_type=jnp.float32) * scale
        )
        allowed = (q_prompt[:, None] == k_prompt[None, :]) & (k_where[None, :] <= q_where[:, None])
        scores = jnp.where(allowed[None], scores, -jnp.inf)
        new_top = jnp.maximum(top, jnp.max(scores, axis=-1, keepdims=True))
        fade = jnp.exp(top - new_top)
        weights = jnp.exp(scores - new_top)
        probs = weights.astype(half_type)
        product = jnp.einsum("hqk,khd->qhd", probs, pair[1], preferred_element_type=jnp.float32)
        accum = accum * jnp.transpose(fade, (1, 0, 2)) + product
        total = total * fade + jnp.sum(weights, axis=-1, keepdims=True)
        return (accum, total, new_top)

    start_state = (
        jnp.zeros((rows, heads_dev, HEAD), jnp.float32),
        jnp.zeros((heads_dev, rows, 1), jnp.float32),
        jnp.full((heads_dev, rows, 1), -jnp.inf, jnp.float32),
    )
    state = online_step(start_state, own_pair, own_first)

    def relay_step(hop, carry):
        carried, running = carry
        carried = passed_along(carried, "dp", 1)
        first = own_first - (hop + 1) * rows
        return (carried, online_step(running, carried, first))

    unused, state = lax.fori_loop(0, reach, relay_step, (own_pair, state))
    accum, total, top = state
    context = (accum / jnp.transpose(total, (1, 0, 2))).astype(half_type).reshape(rows, narrow)
    by_rows = lax.all_gather(w_out.astype(half_type), "dp", axis=0, tiled=True)
    server_out = lax.all_to_all(by_rows, "mp", split_axis=0, concat_axis=1, tiled=True)
    partial_out = jnp.dot(context, server_out, preferred_element_type=jnp.float32)
    attended = lax.psum(partial_out.astype(jnp.bfloat16), "mp").astype(jnp.float32)
    mixed = (tokens.astype(jnp.float32) + attended).astype(half_type)
    normed_two = layer_norm(mixed).astype(half_type)
    units = w_gate.shape[1]
    gate_up = row_product(
        normed_two,
        (
            lax.all_gather(w_gate.astype(half_type), "dp", axis=0, tiled=True),
            lax.all_gather(w_up.astype(half_type), "dp", axis=0, tiled=True),
        ),
    )
    hidden = (jax.nn.silu(gate_up[:, :units]) * gate_up[:, units:]).astype(half_type)
    gathered_down = lax.all_gather(w_down.astype(half_type), "dp", axis=0, tiled=True)
    slab = rows // lax.axis_size("mp")
    server_down = lax.all_to_all(gathered_down, "mp", split_axis=0, concat_axis=1, tiled=True)
    share = lax.psum_scatter(
        jnp.dot(hidden, server_down, preferred_element_type=jnp.float32).astype(jnp.bfloat16),
        "mp",
        scatter_dimension=0,
        tiled=True,
    ).astype(jnp.float32)
    own_rows = lax.dynamic_slice_in_dim(mixed, mp_index * slab, slab, 0)
    return (own_rows.astype(jnp.float32) + share).astype(half_type)


def solution(mesh):
    in_specs = (
        P("dp", None),
        P(),
        P("dp", "mp"),
        P("dp", "mp"),
        P("dp", "mp"),
        P("dp", "mp"),
        P("dp", "mp"),
        P("dp", "mp"),
        P("dp", "mp"),
    )
    out_specs = P(("dp", "mp"), None)
    return jax.shard_map(
        on_device, mesh=mesh, in_specs=in_specs, out_specs=out_specs, check_vma=False
    )
```

profile of v0, /device:TPU:1, one launch (start us, length us, event | category | flops | bytes accessed | tf_op | source)
XLA Modules:
  0.0 904.7 jit_solution(11053108783286988303)
XLA Ops:
  17.0 66.0 %all-gather.10.cloned.1.call-done = bf16[2048,512]{1,0:T(8,128)(2,1)} async-done(((bf16[64,512]{1,0:T(8,128)(2,1)}), bf16[2048,512]{1,0:T(8,128)(2,1)}) %all-gather.10.cloned.1.call-update) | async-done | bytes 2097168 | tf_op jit(solution)/shard_map/all_gather | solution.py:66
  83.0 72.1 %all-gather.12.cloned.1.call-done = bf16[2048,512]{1,0:T(8,128)(2,1)} async-done(((bf16[64,512]{1,0:T(8,128)(2,1)}), bf16[2048,512]{1,0:T(8,128)(2,1)}) %all-gather.12.cloned.1.call-update) | async-done | bytes 2097168 | tf_op jit(solution)/shard_map/all_gather | solution.py:67
  155.2 72.1 %all-gather.8.cloned.1.call-done = bf16[2048,512]{1,0:T(8,128)(2,1)} async-done(((bf16[64,512]{1,0:T(8,128)(2,1)}), bf16[2048,512]{1,0:T(8,128)(2,1)}) %all-gather.8.cloned.1.call-update) | async-done | bytes 2097168 | tf_op jit(solution)/shard_map/all_gather | solution.py:65
  227.3 5.2 fusion.13
  236.4 62.8 %all-gather.14.cloned.1.call-done = bf16[2048,512]{1,0:T(8,128)(2,1)} async-done(((bf16[64,512]{1,0:T(8,128)(2,1)}), bf16[2048,512]{1,0:T(8,128)(2,1)}) %all-gather.14.cloned.1.call-update) | async-done | bytes 2097168 | tf_op jit(solution)/shard_map/all_gather | solution.py:112
  299.2 6.5 all-to-all-start
  305.9 281.6 %while.23 = (s32[]{:T(128)}, bf16[2,256,4,128]{3,1,2,0:T(8,128)(2,1)S(1)}, f32[256,4,128]{2,0,1:T(8,128)S(1)}, f32[4,256,1]{1,0,2:T(4,128)S(1)}, f32[4,256,1]{1,...) while((s32[]{:T(128)}, ...), condition=%wide.region_11.12_spmd.clone.clone, body=%wide.region_7.11_spmd.clone.clone.sunk | while | flops 136518656 | bytes 8333513 | solution.py:109
  305.9 2.2 collective-permute-start
  308.4 36.2 %collective-permute-done = bf16[2,256,4,128]{3,1,2,0:T(8,128)(2,1)S(1)} collective-permute-done((bf16[2,256,4,128]{3,1,2,0:T(8,128)(2,1)S(1)}, bf16[2,256,4,128]{3,1,2,0:T(8,128)(2,1)S(1)}, u32[]{:S(2)}, u32[]{:S(2)}) %collective-permute-start) | collective-permute-done | bytes 524320 | tf_op jit(solution)/shard_map/while/body/eval_jaxpr/ppermute | solution.py:14
  345.6 5.6 collective-permute-start
  351.5 14.5 %collective-permute-done = bf16[2,256,4,128]{3,1,2,0:T(8,128)(2,1)S(1)} collective-permute-done((bf16[2,256,4,128]{3,1,2,0:T(8,128)(2,1)S(1)}, bf16[2,256,4,128]{3,1,2,0:T(8,128)(2,1)S(1)}, u32[]{:S(2)}, u32[]{:S(2)}) %collective-permute-start) | collective-permute-done | bytes 524320 | tf_op jit(solution)/shard_map/while/body/eval_jaxpr/ppermute | solution.py:14
  367.1 5.7 collective-permute-start
  373.1 14.8 %collective-permute-done = bf16[2,256,4,128]{3,1,2,0:T(8,128)(2,1)S(1)} collective-permute-done((bf16[2,256,4,128]{3,1,2,0:T(8,128)(2,1)S(1)}, bf16[2,256,4,128]{3,1,2,0:T(8,128)(2,1)S(1)}, u32[]{:S(2)}, u32[]{:S(2)}) %collective-permute-start) | collective-permute-done | bytes 524320 | tf_op jit(solution)/shard_map/while/body/eval_jaxpr/ppermute | solution.py:14
  389.0 5.7 collective-permute-start
  395.0 9.3 %collective-permute-done = bf16[2,256,4,128]{3,1,2,0:T(8,128)(2,1)S(1)} collective-permute-done((bf16[2,256,4,128]{3,1,2,0:T(8,128)(2,1)S(1)}, bf16[2,256,4,128]{3,1,2,0:T(8,128)(2,1)S(1)}, u32[]{:S(2)}, u32[]{:S(2)}) %collective-permute-start) | collective-permute-done | bytes 524320 | tf_op jit(solution)/shard_map/while/body/eval_jaxpr/ppermute | solution.py:14
  405.4 5.6 collective-permute-start
  411.3 8.4 collective-permute-done
  420.7 5.6 collective-permute-start
  426.6 7.4 collective-permute-done
  435.1 5.6 collective-permute-start
  441.0 6.5 collective-permute-done
  448.5 5.6 collective-permute-start
  454.5 5.8 collective-permute-done
  461.3 6.2 collective-permute-start
  467.8 5.8 collective-permute-done
  474.7 6.2 collective-permute-start
  481.2 5.8 collective-permute-done
  488.0 6.2 collective-permute-start
  494.6 6.1 collective-permute-done
  501.7 6.5 collective-permute-start
  508.5 7.2 collective-permute-done
  516.8 6.5 collective-permute-start
  523.6 8.3 collective-permute-done
  532.9 6.5 collective-permute-start
  539.7 9.4 %collective-permute-done = bf16[2,256,4,128]{3,1,2,0:T(8,128)(2,1)S(1)} collective-permute-done((bf16[2,256,4,128]{3,1,2,0:T(8,128)(2,1)S(1)}, bf16[2,256,4,128]{3,1,2,0:T(8,128)(2,1)S(1)}, u32[]{:S(2)}, u32[]{:S(2)}) %collective-permute-start) | collective-permute-done | bytes 524320 | tf_op jit(solution)/shard_map/while/body/eval_jaxpr/ppermute | solution.py:14
  550.1 6.5 collective-permute-start
  557.0 10.5 %collective-permute-done = bf16[2,256,4,128]{3,1,2,0:T(8,128)(2,1)S(1)} collective-permute-done((bf16[2,256,4,128]{3,1,2,0:T(8,128)(2,1)S(1)}, bf16[2,256,4,128]{3,1,2,0:T(8,128)(2,1)S(1)}, u32[]{:S(2)}, u32[]{:S(2)}) %collective-permute-start) | collective-permute-done | bytes 524320 | tf_op jit(solution)/shard_map/while/body/eval_jaxpr/ppermute | solution.py:14
  568.5 6.5 collective-permute-start
  575.3 11.2 %collective-permute-done = bf16[2,256,4,128]{3,1,2,0:T(8,128)(2,1)S(1)} collective-permute-done((bf16[2,256,4,128]{3,1,2,0:T(8,128)(2,1)S(1)}, bf16[2,256,4,128]{3,1,2,0:T(8,128)(2,1)S(1)}, u32[]{:S(2)}, u32[]{:S(2)}) %collective-permute-start) | collective-permute-done | bytes 524320 | tf_op jit(solution)/shard_map/while/body/eval_jaxpr/ppermute | solution.py:14
  587.8 2.8 copy.43
  595.8 19.7 %all-to-all-start.1 = ((bf16[4,1024,512]{2,1,0:T(8,128)(2,1)}), bf16[4,1024,512]{2,1,0:T(8,128)(2,1)}, u32[]{:S(2)}, u32[]{:S(2)}) async-start(bf16[4,1024,512]{2,1,0:T(8,128)(2,1)} %bitcast.82), calls=%async_computation.1 | async-start | bytes 8388608 | tf_op jit(solution)/shard_map/all_to_all | solution.py:129
  615.4 67.1 %all-reduce.2.cloned.1.call-done = bf16[256,2048]{1,0:T(8,128)(2,1)} async-done(((bf16[256,2048]{1,0:T(8,128)(2,1)}), bf16[256,2048]{1,0:T(8,128)(2,1)}) %all-reduce.2.cloned.1.call-update) | async-done | bytes 1048592 | tf_op jit(solution)/shard_map/psum | solution.py:115
  684.6 90.4 %all-gather.16.cloned.1.call-done = bf16[2048,1024]{1,0:T(8,128)(2,1)} async-done(((bf16[64,1024]{1,0:T(8,128)(2,1)}), bf16[2048,1024]{1,0:T(8,128)(2,1)}) %all-gather.16.cloned.1.call-update) | async-done | bytes 4194320 | tf_op jit(solution)/shard_map/all_gather | solution.py:122
  775.0 82.9 %all-gather.18.cloned.1.call-done = bf16[2048,1024]{1,0:T(8,128)(2,1)} async-done(((bf16[64,1024]{1,0:T(8,128)(2,1)}), bf16[2048,1024]{1,0:T(8,128)(2,1)}) %all-gather.18.cloned.1.call-update) | async-done | bytes 4194320 | tf_op jit(solution)/shard_map/all_gather | solution.py:123
  857.9 7.2 fusion.9
  865.1 6.3 copy.44
  871.4 5.1 convolution_convert_fusion.1
  876.5 19.9 %reduce-scatter.2.cloned.1.call-done = bf16[64,2048]{1,0:T(8,128)(2,1)} async-done(((bf16[256,2048]{1,0:T(8,128)(2,1)}), bf16[64,2048]{1,0:T(8,128)(2,1)}) %reduce-scatter.2.cloned.1.call-update) | async-done | bytes 262160 | tf_op jit(solution)/shard_map/reduce_scatter | solution.py:130
  (240 shorter events, 43.3 us)
Async XLA Ops:
  6.5 9.7 %copy-start.1 = (s32[4]{0:T(128)S(1)}, s32[4]{0:T(128)}, u32[]{:S(2)}) copy-start(s32[4]{0:T(128)} %param.12) | copy-start | bytes 52
  6.5 9.0 %copy-start = (bf16[256,2048]{1,0:T(8,128)(2,1)S(1)}, bf16[256,2048]{1,0:T(8,128)(2,1)}, u32[]{:S(2)}) copy-start(bf16[256,2048]{1,0:T(8,128)(2,1)} %param.11) | copy-start | bytes 3145732
  6.5 76.5 %all-gather.10.cloned.1.call-start = ((), (), s32[]{:S(2)}) async-start(), calls=%async_computation.4 | async-start | bytes 2162688 | tf_op jit(solution)/shard_map/all_gather | solution.py:66
  8.2 147.0 %all-gather.12.cloned.1.call-start = ((), (), s32[]{:S(2)}) async-start(), calls=%async_computation.5 | async-start | bytes 2162688 | tf_op jit(solution)/shard_map/all_gather | solution.py:67
  9.8 217.5 %all-gather.8.cloned.1.call-start = ((), (), s32[]{:S(2)}) async-start(), calls=%async_computation.3 | async-start | bytes 2162688 | tf_op jit(solution)/shard_map/all_gather | solution.py:65
  11.4 287.8 %all-gather.14.cloned.1.call-start = ((), (), s32[]{:S(2)}) async-start(), calls=%async_computation.6 | async-start | bytes 2162688 | tf_op jit(solution)/shard_map/all_gather | solution.py:112
  13.0 582.8 %all-gather.20.cloned.1.call-start = ((), (), s32[]{:S(2)}) async-start(), calls=%async_computation.10 | async-start | bytes 4325376 | tf_op jit(solution)/shard_map/all_gather | solution.py:127
  299.2 288.6 %all-to-all-start = ((bf16[4,512,512]{2,1,0:T(8,128)(2,1)}), bf16[4,512,512]{2,1,0:T(8,128)(2,1)}, u32[]{:S(2)}, u32[]{:S(2)}) async-start(bf16[4,512,512]{2,1,0:T(8,128)(2,1)} %bitcast.88), calls=%async_computation | async-start | bytes 4194304 | tf_op jit(solution)/shard_map/all_to_all | solution.py:113
  305.7 376.8 %all-reduce.2.cloned.1.call-start = ((), (), s32[]{:S(2)}) async-start(), calls=%async_computation.7 | async-start | bytes 2097152 | tf_op jit(solution)/shard_map/psum | solution.py:115
  305.9 38.7 %collective-permute-start = (bf16[2,256,4,128]{3,1,2,0:T(8,128)(2,1)S(1)}, bf16[2,256,4,128]{3,1,2,0:T(8,128)(2,1)S(1)}, u32[]{:S(2)}, u32[]{:S(2)}) collective-permute-start(bf16[2,256,4,128]{3,1,2,0:T(8,128)(2,1)S(1)} %get-tuple-element.447), channel_id=1, source_target_pairs={{0,4},{4,8},{8,12},{12,16},{16,20},{20,24},{24,28},{28,32},{32,36}... | collective-permute-start | bytes 1572872 | tf_op jit(solution)/shard_map/while/body/eval_jaxpr/ppermute | solution.py:14
  345.6 20.4 %collective-permute-start = (bf16[2,256,4,128]{3,1,2,0:T(8,128)(2,1)S(1)}, bf16[2,256,4,128]{3,1,2,0:T(8,128)(2,1)S(1)}, u32[]{:S(2)}, u32[]{:S(2)}) collective-permute-start(bf16[2,256,4,128]{3,1,2,0:T(8,128)(2,1)S(1)} %get-tuple-element.447), channel_id=1, source_target_pairs={{0,4},{4,8},{8,12},{12,16},{16,20},{20,24},{24,28},{28,32},{32,36}... | collective-permute-start | bytes 1572872 | tf_op jit(solution)/shard_map/while/body/eval_jaxpr/ppermute | solution.py:14
  367.1 20.9 %collective-permute-start = (bf16[2,256,4,128]{3,1,2,0:T(8,128)(2,1)S(1)}, bf16[2,256,4,128]{3,1,2,0:T(8,128)(2,1)S(1)}, u32[]{:S(2)}, u32[]{:S(2)}) collective-permute-start(bf16[2,256,4,128]{3,1,2,0:T(8,128)(2,1)S(1)} %get-tuple-element.447), channel_id=1, source_target_pairs={{0,4},{4,8},{8,12},{12,16},{16,20},{20,24},{24,28},{28,32},{32,36}... | collective-permute-start | bytes 1572872 | tf_op jit(solution)/shard_map/while/body/eval_jaxpr/ppermute | solution.py:14
  389.0 15.3 %collective-permute-start = (bf16[2,256,4,128]{3,1,2,0:T(8,128)(2,1)S(1)}, bf16[2,256,4,128]{3,1,2,0:T(8,128)(2,1)S(1)}, u32[]{:S(2)}, u32[]{:S(2)}) collective-permute-start(bf16[2,256,4,128]{3,1,2,0:T(8,128)(2,1)S(1)} %get-tuple-element.447), channel_id=1, source_target_pairs={{0,4},{4,8},{8,12},{12,16},{16,20},{20,24},{24,28},{28,32},{32,36}... | collective-permute-start | bytes 1572872 | tf_op jit(solution)/shard_map/while/body/eval_jaxpr/ppermute | solution.py:14
  405.4 14.3 %collective-permute-start = (bf16[2,256,4,128]{3,1,2,0:T(8,128)(2,1)S(1)}, bf16[2,256,4,128]{3,1,2,0:T(8,128)(2,1)S(1)}, u32[]{:S(2)}, u32[]{:S(2)}) collective-permute-start(bf16[2,256,4,128]{3,1,2,0:T(8,128)(2,1)S(1)} %get-tuple-element.447), channel_id=1, source_target_pairs={{0,4},{4,8},{8,12},{12,16},{16,20},{20,24},{24,28},{28,32},{32,36}... | collective-permute-start | bytes 1572872 | tf_op jit(solution)/shard_map/while/body/eval_jaxpr/ppermute | solution.py:14
  420.7 13.3 %collective-permute-start = (bf16[2,256,4,128]{3,1,2,0:T(8,128)(2,1)S(1)}, bf16[2,256,4,128]{3,1,2,0:T(8,128)(2,1)S(1)}, u32[]{:S(2)}, u32[]{:S(2)}) collective-permute-start(bf16[2,256,4,128]{3,1,2,0:T(8,128)(2,1)S(1)} %get-tuple-element.447), channel_id=1, source_target_pairs={{0,4},{4,8},{8,12},{12,16},{16,20},{20,24},{24,28},{28,32},{32,36}... | collective-permute-start | bytes 1572872 | tf_op jit(solution)/shard_map/while/body/eval_jaxpr/ppermute | solution.py:14
  435.1 12.4 %collective-permute-start = (bf16[2,256,4,128]{3,1,2,0:T(8,128)(2,1)S(1)}, bf16[2,256,4,128]{3,1,2,0:T(8,128)(2,1)S(1)}, u32[]{:S(2)}, u32[]{:S(2)}) collective-permute-start(bf16[2,256,4,128]{3,1,2,0:T(8,128)(2,1)S(1)} %get-tuple-element.447), channel_id=1, source_target_pairs={{0,4},{4,8},{8,12},{12,16},{16,20},{20,24},{24,28},{28,32},{32,36}... | collective-permute-start | bytes 1572872 | tf_op jit(solution)/shard_map/while/body/eval_jaxpr/ppermute | solution.py:14
  448.5 11.7 %collective-permute-start = (bf16[2,256,4,128]{3,1,2,0:T(8,128)(2,1)S(1)}, bf16[2,256,4,128]{3,1,2,0:T(8,128)(2,1)S(1)}, u32[]{:S(2)}, u32[]{:S(2)}) collective-permute-start(bf16[2,256,4,128]{3,1,2,0:T(8,128)(2,1)S(1)} %get-tuple-element.447), channel_id=1, source_target_pairs={{0,4},{4,8},{8,12},{12,16},{16,20},{20,24},{24,28},{28,32},{32,36}... | collective-permute-start | bytes 1572872 | tf_op jit(solution)/shard_map/while/body/eval_jaxpr/ppermute | solution.py:14
  461.3 12.3 %collective-permute-start = (bf16[2,256,4,128]{3,1,2,0:T(8,128)(2,1)S(1)}, bf16[2,256,4,128]{3,1,2,0:T(8,128)(2,1)S(1)}, u32[]{:S(2)}, u32[]{:S(2)}) collective-permute-start(bf16[2,256,4,128]{3,1,2,0:T(8,128)(2,1)S(1)} %get-tuple-element.447), channel_id=1, source_target_pairs={{0,4},{4,8},{8,12},{12,16},{16,20},{20,24},{24,28},{28,32},{32,36}... | collective-permute-start | bytes 1572872 | tf_op jit(solution)/shard_map/while/body/eval_jaxpr/ppermute | solution.py:14
  474.7 12.3 %collective-permute-start = (bf16[2,256,4,128]{3,1,2,0:T(8,128)(2,1)S(1)}, bf16[2,256,4,128]{3,1,2,0:T(8,128)(2,1)S(1)}, u32[]{:S(2)}, u32[]{:S(2)}) collective-permute-start(bf16[2,256,4,128]{3,1,2,0:T(8,128)(2,1)S(1)} %get-tuple-element.447), channel_id=1, source_target_pairs={{0,4},{4,8},{8,12},{12,16},{16,20},{20,24},{24,28},{28,32},{32,36}... | collective-permute-start | bytes 1572872 | tf_op jit(solution)/shard_map/while/body/eval_jaxpr/ppermute | solution.py:14
  488.0 12.6 %collective-permute-start = (bf16[2,256,4,128]{3,1,2,0:T(8,128)(2,1)S(1)}, bf16[2,256,4,128]{3,1,2,0:T(8,128)(2,1)S(1)}, u32[]{:S(2)}, u32[]{:S(2)}) collective-permute-start(bf16[2,256,4,128]{3,1,2,0:T(8,128)(2,1)S(1)} %get-tuple-element.447), channel_id=1, source_target_pairs={{0,4},{4,8},{8,12},{12,16},{16,20},{20,24},{24,28},{28,32},{32,36}... | collective-permute-start | bytes 1572872 | tf_op jit(solution)/shard_map/while/body/eval_jaxpr/ppermute | solution.py:14
  501.7 14.0 %collective-permute-start = (bf16[2,256,4,128]{3,1,2,0:T(8,128)(2,1)S(1)}, bf16[2,256,4,128]{3,1,2,0:T(8,128)(2,1)S(1)}, u32[]{:S(2)}, u32[]{:S(2)}) collective-permute-start(bf16[2,256,4,128]{3,1,2,0:T(8,128)(2,1)S(1)} %get-tuple-element.447), channel_id=1, source_target_pairs={{0,4},{4,8},{8,12},{12,16},{16,20},{20,24},{24,28},{28,32},{32,36}... | collective-permute-start | bytes 1572872 | tf_op jit(solution)/shard_map/while/body/eval_jaxpr/ppermute | solution.py:14
  516.8 15.1 %collective-permute-start = (bf16[2,256,4,128]{3,1,2,0:T(8,128)(2,1)S(1)}, bf16[2,256,4,128]{3,1,2,0:T(8,128)(2,1)S(1)}, u32[]{:S(2)}, u32[]{:S(2)}) collective-permute-start(bf16[2,256,4,128]{3,1,2,0:T(8,128)(2,1)S(1)} %get-tuple-element.447), channel_id=1, source_target_pairs={{0,4},{4,8},{8,12},{12,16},{16,20},{20,24},{24,28},{28,32},{32,36}... | collective-permute-start | bytes 1572872 | tf_op jit(solution)/shard_map/while/body/eval_jaxpr/ppermute | solution.py:14
  532.9 16.2 %collective-permute-start = (bf16[2,256,4,128]{3,1,2,0:T(8,128)(2,1)S(1)}, bf16[2,256,4,128]{3,1,2,0:T(8,128)(2,1)S(1)}, u32[]{:S(2)}, u32[]{:S(2)}) collective-permute-start(bf16[2,256,4,128]{3,1,2,0:T(8,128)(2,1)S(1)} %get-tuple-element.447), channel_id=1, source_target_pairs={{0,4},{4,8},{8,12},{12,16},{16,20},{20,24},{24,28},{28,32},{32,36}... | collective-permute-start | bytes 1572872 | tf_op jit(solution)/shard_map/while/body/eval_jaxpr/ppermute | solution.py:14
  550.1 17.3 %collective-permute-start = (bf16[2,256,4,128]{3,1,2,0:T(8,128)(2,1)S(1)}, bf16[2,256,4,128]{3,1,2,0:T(8,128)(2,1)S(1)}, u32[]{:S(2)}, u32[]{:S(2)}) collective-permute-start(bf16[2,256,4,128]{3,1,2,0:T(8,128)(2,1)S(1)} %get-tuple-element.447), channel_id=1, source_target_pairs={{0,4},{4,8},{8,12},{12,16},{16,20},{20,24},{24,28},{28,32},{32,36}... | collective-permute-start | bytes 1572872 | tf_op jit(solution)/shard_map/while/body/eval_jaxpr/ppermute | solution.py:14
  568.5 18.0 %collective-permute-start = (bf16[2,256,4,128]{3,1,2,0:T(8,128)(2,1)S(1)}, bf16[2,256,4,128]{3,1,2,0:T(8,128)(2,1)S(1)}, u32[]{:S(2)}, u32[]{:S(2)}) collective-permute-start(bf16[2,256,4,128]{3,1,2,0:T(8,128)(2,1)S(1)} %get-tuple-element.447), channel_id=1, source_target_pairs={{0,4},{4,8},{8,12},{12,16},{16,20},{20,24},{24,28},{28,32},{32,36}... | collective-permute-start | bytes 1572872 | tf_op jit(solution)/shard_map/while/body/eval_jaxpr/ppermute | solution.py:14
  592.4 182.6 %all-gather.16.cloned.1.call-start = ((), (), s32[]{:S(2)}) async-start(), calls=%async_computation.8 | async-start | bytes 4325376 | tf_op jit(solution)/shard_map/all_gather | solution.py:122
  594.1 263.8 %all-gather.18.cloned.1.call-start = ((), (), s32[]{:S(2)}) async-start(), calls=%async_computation.9 | async-start | bytes 4325376 | tf_op jit(solution)/shard_map/all_gather | solution.py:123
  595.8 269.3 %all-to-all-start.1 = ((bf16[4,1024,512]{2,1,0:T(8,128)(2,1)}), bf16[4,1024,512]{2,1,0:T(8,128)(2,1)}, u32[]{:S(2)}, u32[]{:S(2)}) async-start(bf16[4,1024,512]{2,1,0:T(8,128)(2,1)} %bitcast.82), calls=%async_computation.1 | async-start | bytes 8388608 | tf_op jit(solution)/shard_map/all_to_all | solution.py:129
  615.4 281.0 %reduce-scatter.2.cloned.1.call-start = ((), (), s32[]{:S(2)}) async-start(), calls=%async_computation.11 | async-start | bytes 1310720 | tf_op jit(solution)/shard_map/reduce_scatter | solution.py:130
Sparse Core Ops, SparseCore 0:
  10.5 72.4 all-gather.9
  86.2 68.9 all-gather.11
  158.3 68.9 all-gather.7
  230.3 68.9 all-gather.13
  302.1 91.9 all-gather.19
  592.5 89.9 all-reduce.1
  686.1 88.8 all-gather.15
  778.5 79.3 all-gather.17
  876.7 19.7 reduce-scatter.1
where the time goes:
time: 906 us; the launch traced here: 905 us
  waiting for transfers between devices  701 us (77%)
  starting transfers between devices  120 us (13%)
  matrix products  32.3 us (4%)
  other arithmetic  24.8 us (3%)
  between operations  13.4 us (1%)
  local copies, waits for them, and re-layouts  12.3 us (1%)
    ppermute x16, waiting for transfers between devices, passed_along(): lax.ppermute(value, axis, [(source, source + steps) for source in range(i...  167 us
    ppermute x16, starting transfers between devices, passed_along(): lax.ppermute(value, axis, [(source, source + steps) for source in range(i...  93.3 us
    all_gather x1, waiting for transfers between devices, on_device(): lax.all_gather(w_gate.astype(half_type), 'dp', axis=0, tiled=True)  90.4 us
    all_gather x1, waiting for transfers between devices, on_device(): lax.all_gather(w_up.astype(half_type), 'dp', axis=0, tiled=True)  82.9 us
    all_gather x1, waiting for transfers between devices, on_device(): lax.all_gather(w_query.astype(half_type), 'dp', axis=0, tiled=True)  72.1 us
    all_gather x1, waiting for transfers between devices, on_device(): lax.all_gather(w_value.astype(half_type), 'dp', axis=0, tiled=True)  72.1 us
    psum x1, waiting for transfers between devices, on_device(): lax.psum(partial_out.astype(jnp.bfloat16), 'mp').astype(jnp.float32)  67.1 us
    all_gather x1, waiting for transfers between devices, on_device(): lax.all_gather(w_key.astype(half_type), 'dp', axis=0, tiled=True)  66 us
  transfers between devices with their start and end apart: 27, of which 24 were waited for; matrix products, arithmetic and copies ran while one was open for 6% of the time, Pallas kernels for 0%

commit v1 on v0

--- a/solution.py
+++ b/solution.py
@@ -64,7 +64,12 @@
         (
             lax.all_gather(w_query.astype(half_type), "dp", axis=0, tiled=True),
             lax.all_gather(w_key.astype(half_type), "dp", axis=0, tiled=True),
-            lax.all_gather(w_value.astype(half_type), "dp", axis=0, tiled=True),
+            jnp.concatenate(
+                lax.all_to_all(
+                    jnp.stack([w_value.astype(half_type)] * lax.axis_size("dp"), axis=0), "dp", 0, 0
+                ),
+                0,
+            ),
         ),
     )
     q_prompt, q_offset, q_where = prompt_coords(dp_index * rows, rows, lengths)

time: 906 us -> 851 us (0.939)
  waiting for transfers between devices: 701 us -> 635 us
  starting transfers between devices: 120 us -> 131 us
    all_gather x1 -> x0, waiting for transfers between devices: 72.1 us -> none  [on_device(): lax.all_gather(w_value.astype(half_type), 'dp', axis=0, tiled=True)]
    all_gather x1, waiting for transfers between devices: 72.1 us -> 43.1 us  [on_device(): lax.all_gather(w_query.astype(half_type), 'dp', axis=0, tiled=True)]
    all_to_all x0 -> x1, waiting for transfers between devices: none -> 28.9 us  [on_device(): lax.all_to_all(jnp.stack([w_value.astype(half_type)] * lax.axis_size('dp'...]
    all_to_all x0 -> x1, starting transfers between devices: none -> 11.5 us  [on_device(): lax.all_to_all(jnp.stack([w_value.astype(half_type)] * lax.axis_size('dp'...]
where the time goes in v1:
time: 851 us; the launch traced here: 850 us
  waiting for transfers between devices  635 us (75%)
  starting transfers between devices  131 us (15%)
  matrix products  32.3 us (4%)
  other arithmetic  22.5 us (3%)
  local copies, waits for them, and re-layouts  13.9 us (2%)
  between operations  13.7 us (2%)
    ppermute x16, waiting for transfers between devices, passed_along(): lax.ppermute(value, axis, [(source, source + steps) for source in range(i...  167 us
    ppermute x16, starting transfers between devices, passed_along(): lax.ppermute(value, axis, [(source, source + steps) for source in range(i...  93.3 us
    all_gather x1, waiting for transfers between devices, on_device(): lax.all_gather(w_gate.astype(half_type), 'dp', axis=0, tiled=True)  90.3 us
    all_gather x1, waiting for transfers between devices, on_device(): lax.all_gather(w_up.astype(half_type), 'dp', axis=0, tiled=True)  82.9 us
    all_gather x1, waiting for transfers between devices, on_device(): lax.all_gather(w_key.astype(half_type), 'dp', axis=0, tiled=True)  72.1 us
    psum x1, waiting for transfers between devices, on_device(): lax.psum(partial_out.astype(jnp.bfloat16), 'mp').astype(jnp.float32)  67.1 us
    all_gather x1, waiting for transfers between devices, on_device(): by_rows = lax.all_gather(w_out.astype(half_type), 'dp', axis=0, tiled=True)  63 us
    all_gather x1, waiting for transfers between devices, on_device(): lax.all_gather(w_query.astype(half_type), 'dp', axis=0, tiled=True)  43.1 us
  transfers between devices with their start and end apart: 27, of which 24 were waited for; matrix products, arithmetic and copies ran while one was open for 6% of the time, Pallas kernels for 0%

profile of v1, /device:TPU:1, one launch (start us, length us, event | category | flops | bytes accessed | tf_op | source)
XLA Modules:
  0.0 849.6 jit_solution(9629496919919566374)
XLA Ops:
  13.8 11.5 %all-to-all-start = ((bf16[32,64,512]{2,1,0:T(8,128)(2,1)}), bf16[32,64,512]{2,1,0:T(8,128)(2,1)S(1)}, u32[]{:S(2)}, u32[]{:S(2)}) async-start(bf16[32,64,512]{2,1,0:T(8,128)(2,1)} %stack.4), calls=%async_computation | async-start | bytes 4194304 | tf_op jit(solution)/shard_map/all_to_all | solution.py:68
  27.7 28.9 %all-to-all-done = bf16[32,64,512]{2,1,0:T(8,128)(2,1)S(1)} async-done(((bf16[32,64,512]{2,1,0:T(8,128)(2,1)}), bf16[32,64,512]{2,1,0:T(8,128)(2,1)S(1)}, u32[]{:S(2)}, u32[]{:S(2)}) %all-to-all-start) | async-done | bytes 2097184 | tf_op jit(solution)/shard_map/all_to_all | solution.py:68
  56.6 43.1 %all-gather.7.cloned.1.call-done = bf16[2048,512]{1,0:T(8,128)(2,1)} async-done(((bf16[64,512]{1,0:T(8,128)(2,1)}), bf16[2048,512]{1,0:T(8,128)(2,1)}) %all-gather.7.cloned.1.call-update) | async-done | bytes 2097168 | tf_op jit(solution)/shard_map/all_gather | solution.py:65
  99.7 72.1 %all-gather.9.cloned.1.call-done = bf16[2048,512]{1,0:T(8,128)(2,1)} async-done(((bf16[64,512]{1,0:T(8,128)(2,1)}), bf16[2048,512]{1,0:T(8,128)(2,1)}) %all-gather.9.cloned.1.call-update) | async-done | bytes 2097168 | tf_op jit(solution)/shard_map/all_gather | solution.py:66
  171.8 5.2 fusion.13
  180.9 63.0 %all-gather.11.cloned.1.call-done = bf16[2048,512]{1,0:T(8,128)(2,1)} async-done(((bf16[64,512]{1,0:T(8,128)(2,1)}), bf16[2048,512]{1,0:T(8,128)(2,1)}) %all-gather.11.cloned.1.call-update) | async-done | bytes 2097168 | tf_op jit(solution)/shard_map/all_gather | solution.py:117
  243.9 6.5 all-to-all-start.1
  250.6 281.6 %while.23 = (s32[]{:T(128)}, bf16[2,256,4,128]{3,1,2,0:T(8,128)(2,1)S(1)}, f32[256,4,128]{2,0,1:T(8,128)S(1)}, f32[4,256,1]{1,0,2:T(4,128)S(1)}, f32[4,256,1]{1,...) while((s32[]{:T(128)}, ...), condition=%wide.region_11.12_spmd.clone.clone, body=%wide.region_7.11_spmd.clone.clone.sunk | while | flops 136518656 | bytes 8333513 | solution.py:114
  253.1 36.2 %collective-permute-done = bf16[2,256,4,128]{3,1,2,0:T(8,128)(2,1)S(1)} collective-permute-done((bf16[2,256,4,128]{3,1,2,0:T(8,128)(2,1)S(1)}, bf16[2,256,4,128]{3,1,2,0:T(8,128)(2,1)S(1)}, u32[]{:S(2)}, u32[]{:S(2)}) %collective-permute-start) | collective-permute-done | bytes 524320 | tf_op jit(solution)/shard_map/while/body/eval_jaxpr/ppermute | solution.py:14
  290.3 5.6 collective-permute-start
  296.2 14.5 %collective-permute-done = bf16[2,256,4,128]{3,1,2,0:T(8,128)(2,1)S(1)} collective-permute-done((bf16[2,256,4,128]{3,1,2,0:T(8,128)(2,1)S(1)}, bf16[2,256,4,128]{3,1,2,0:T(8,128)(2,1)S(1)}, u32[]{:S(2)}, u32[]{:S(2)}) %collective-permute-start) | collective-permute-done | bytes 524320 | tf_op jit(solution)/shard_map/while/body/eval_jaxpr/ppermute | solution.py:14
  311.8 5.8 collective-permute-start
  317.8 14.8 %collective-permute-done = bf16[2,256,4,128]{3,1,2,0:T(8,128)(2,1)S(1)} collective-permute-done((bf16[2,256,4,128]{3,1,2,0:T(8,128)(2,1)S(1)}, bf16[2,256,4,128]{3,1,2,0:T(8,128)(2,1)S(1)}, u32[]{:S(2)}, u32[]{:S(2)}) %collective-permute-start) | collective-permute-done | bytes 524320 | tf_op jit(solution)/shard_map/while/body/eval_jaxpr/ppermute | solution.py:14
  333.7 5.7 collective-permute-start
  339.7 9.3 %collective-permute-done = bf16[2,256,4,128]{3,1,2,0:T(8,128)(2,1)S(1)} collective-permute-done((bf16[2,256,4,128]{3,1,2,0:T(8,128)(2,1)S(1)}, bf16[2,256,4,128]{3,1,2,0:T(8,128)(2,1)S(1)}, u32[]{:S(2)}, u32[]{:S(2)}) %collective-permute-start) | collective-permute-done | bytes 524320 | tf_op jit(solution)/shard_map/while/body/eval_jaxpr/ppermute | solution.py:14
  350.0 5.6 collective-permute-start
  355.9 8.4 collective-permute-done
  365.3 5.6 collective-permute-start
  371.2 7.4 collective-permute-done
  379.7 5.6 collective-permute-start
  385.6 6.5 collective-permute-done
  393.2 5.6 collective-permute-start
  399.1 5.8 collective-permute-done
  406.0 6.2 collective-permute-start
  412.4 5.8 collective-permute-done
  419.3 6.2 collective-permute-start
  425.8 5.8 collective-permute-done
  432.7 6.2 collective-permute-start
  439.2 6.1 collective-permute-done
  446.4 6.5 collective-permute-start
  453.2 7.2 collective-permute-done
  461.4 6.5 collective-permute-start
  468.3 8.3 collective-permute-done
  477.6 6.5 collective-permute-start
  484.4 9.4 %collective-permute-done = bf16[2,256,4,128]{3,1,2,0:T(8,128)(2,1)S(1)} collective-permute-done((bf16[2,256,4,128]{3,1,2,0:T(8,128)(2,1)S(1)}, bf16[2,256,4,128]{3,1,2,0:T(8,128)(2,1)S(1)}, u32[]{:S(2)}, u32[]{:S(2)}) %collective-permute-start) | collective-permute-done | bytes 524320 | tf_op jit(solution)/shard_map/while/body/eval_jaxpr/ppermute | solution.py:14
  494.8 6.5 collective-permute-start
  501.6 10.5 %collective-permute-done = bf16[2,256,4,128]{3,1,2,0:T(8,128)(2,1)S(1)} collective-permute-done((bf16[2,256,4,128]{3,1,2,0:T(8,128)(2,1)S(1)}, bf16[2,256,4,128]{3,1,2,0:T(8,128)(2,1)S(1)}, u32[]{:S(2)}, u32[]{:S(2)}) %collective-permute-start) | collective-permute-done | bytes 524320 | tf_op jit(solution)/shard_map/while/body/eval_jaxpr/ppermute | solution.py:14
  513.1 6.5 collective-permute-start
  519.9 11.2 %collective-permute-done = bf16[2,256,4,128]{3,1,2,0:T(8,128)(2,1)S(1)} collective-permute-done((bf16[2,256,4,128]{3,1,2,0:T(8,128)(2,1)S(1)}, bf16[2,256,4,128]{3,1,2,0:T(8,128)(2,1)S(1)}, u32[]{:S(2)}, u32[]{:S(2)}) %collective-permute-start) | collective-permute-done | bytes 524320 | tf_op jit(solution)/shard_map/while/body/eval_jaxpr/ppermute | solution.py:14
  532.4 2.8 copy.43
  540.4 19.7 %all-to-all-start.2 = ((bf16[4,1024,512]{2,1,0:T(8,128)(2,1)}), bf16[4,1024,512]{2,1,0:T(8,128)(2,1)}, u32[]{:S(2)}, u32[]{:S(2)}) async-start(bf16[4,1024,512]{2,1,0:T(8,128)(2,1)} %bitcast.83), calls=%async_computation.2 | async-start | bytes 8388608 | tf_op jit(solution)/shard_map/all_to_all | solution.py:134
  560.1 67.1 %all-reduce.2.cloned.1.call-done = bf16[256,2048]{1,0:T(8,128)(2,1)} async-done(((bf16[256,2048]{1,0:T(8,128)(2,1)}), bf16[256,2048]{1,0:T(8,128)(2,1)}) %all-reduce.2.cloned.1.call-update) | async-done | bytes 1048592 | tf_op jit(solution)/shard_map/psum | solution.py:120
  629.2 90.3 %all-gather.13.cloned.1.call-done = bf16[2048,1024]{1,0:T(8,128)(2,1)} async-done(((bf16[64,1024]{1,0:T(8,128)(2,1)}), bf16[2048,1024]{1,0:T(8,128)(2,1)}) %all-gather.13.cloned.1.call-update) | async-done | bytes 4194320 | tf_op jit(solution)/shard_map/all_gather | solution.py:127
  719.5 82.9 %all-gather.15.cloned.1.call-done = bf16[2048,1024]{1,0:T(8,128)(2,1)} async-done(((bf16[64,1024]{1,0:T(8,128)(2,1)}), bf16[2048,1024]{1,0:T(8,128)(2,1)}) %all-gather.15.cloned.1.call-update) | async-done | bytes 4194320 | tf_op jit(solution)/shard_map/all_gather | solution.py:128
  802.4 7.2 fusion.9
  809.6 6.3 copy.44
  815.9 5.1 convolution_convert_fusion.1
  821.0 20.1 %reduce-scatter.2.cloned.1.call-done = bf16[64,2048]{1,0:T(8,128)(2,1)} async-done(((bf16[256,2048]{1,0:T(8,128)(2,1)}), bf16[64,2048]{1,0:T(8,128)(2,1)}) %reduce-scatter.2.cloned.1.call-update) | async-done | bytes 262160 | tf_op jit(solution)/shard_map/reduce_scatter | solution.py:135
  (242 shorter events, 44.7 us)
Async XLA Ops:
  6.5 93.1 %all-gather.7.cloned.1.call-start = ((), (), s32[]{:S(2)}) async-start(), calls=%async_computation.4 | async-start | bytes 2162688 | tf_op jit(solution)/shard_map/all_gather | solution.py:65
  8.1 163.7 %all-gather.9.cloned.1.call-start = ((), (), s32[]{:S(2)}) async-start(), calls=%async_computation.5 | async-start | bytes 2162688 | tf_op jit(solution)/shard_map/all_gather | solution.py:66
  9.7 234.2 %all-gather.11.cloned.1.call-start = ((), (), s32[]{:S(2)}) async-start(), calls=%async_computation.6 | async-start | bytes 2162688 | tf_op jit(solution)/shard_map/all_gather | solution.py:117
  13.8 11.5 %copy-start.1 = (f32[128,512]{1,0:T(8,128)S(1)}, f32[128,512]{1,0:T(8,128)}, u32[]{:S(2)}) copy-start(f32[128,512]{1,0:T(8,128)} %param.19) | copy-start | bytes 786436
  13.8 12.3 %copy-start.2 = (s32[4]{0:T(128)S(1)}, s32[4]{0:T(128)}, u32[]{:S(2)}) copy-start(s32[4]{0:T(128)} %param.12) | copy-start | bytes 52
  13.8 12.5 %copy-start = (bf16[256,2048]{1,0:T(8,128)(2,1)S(1)}, bf16[256,2048]{1,0:T(8,128)(2,1)}, u32[]{:S(2)}) copy-start(bf16[256,2048]{1,0:T(8,128)(2,1)} %param.11) | copy-start | bytes 3145732
  13.8 42.8 %all-to-all-start = ((bf16[32,64,512]{2,1,0:T(8,128)(2,1)}), bf16[32,64,512]{2,1,0:T(8,128)(2,1)S(1)}, u32[]{:S(2)}, u32[]{:S(2)}) async-start(bf16[32,64,512]{2,1,0:T(8,128)(2,1)} %stack.4), calls=%async_computation | async-start | bytes 4194304 | tf_op jit(solution)/shard_map/all_to_all | solution.py:68
  25.3 515.2 %all-gather.17.cloned.1.call-start = ((), (), s32[]{:S(2)}) async-start(), calls=%async_computation.10 | async-start | bytes 4325376 | tf_op jit(solution)/shard_map/all_gather | solution.py:132
  243.9 288.6 %all-to-all-start.1 = ((bf16[4,512,512]{2,1,0:T(8,128)(2,1)}), bf16[4,512,512]{2,1,0:T(8,128)(2,1)}, u32[]{:S(2)}, u32[]{:S(2)}) async-start(bf16[4,512,512]{2,1,0:T(8,128)(2,1)} %bitcast.89), calls=%async_computation.1 | async-start | bytes 4194304 | tf_op jit(solution)/shard_map/all_to_all | solution.py:118
  250.4 376.8 %all-reduce.2.cloned.1.call-start = ((), (), s32[]{:S(2)}) async-start(), calls=%async_computation.7 | async-start | bytes 2097152 | tf_op jit(solution)/shard_map/psum | solution.py:120
  250.6 38.7 %collective-permute-start = (bf16[2,256,4,128]{3,1,2,0:T(8,128)(2,1)S(1)}, bf16[2,256,4,128]{3,1,2,0:T(8,128)(2,1)S(1)}, u32[]{:S(2)}, u32[]{:S(2)}) collective-permute-start(bf16[2,256,4,128]{3,1,2,0:T(8,128)(2,1)S(1)} %get-tuple-element.447), channel_id=1, source_target_pairs={{0,4},{4,8},{8,12},{12,16},{16,20},{20,24},{24,28},{28,32},{32,36}... | collective-permute-start | bytes 1572872 | tf_op jit(solution)/shard_map/while/body/eval_jaxpr/ppermute | solution.py:14
  290.3 20.4 %collective-permute-start = (bf16[2,256,4,128]{3,1,2,0:T(8,128)(2,1)S(1)}, bf16[2,256,4,128]{3,1,2,0:T(8,128)(2,1)S(1)}, u32[]{:S(2)}, u32[]{:S(2)}) collective-permute-start(bf16[2,256,4,128]{3,1,2,0:T(8,128)(2,1)S(1)} %get-tuple-element.447), channel_id=1, source_target_pairs={{0,4},{4,8},{8,12},{12,16},{16,20},{20,24},{24,28},{28,32},{32,36}... | collective-permute-start | bytes 1572872 | tf_op jit(solution)/shard_map/while/body/eval_jaxpr/ppermute | solution.py:14
  311.8 20.9 %collective-permute-start = (bf16[2,256,4,128]{3,1,2,0:T(8,128)(2,1)S(1)}, bf16[2,256,4,128]{3,1,2,0:T(8,128)(2,1)S(1)}, u32[]{:S(2)}, u32[]{:S(2)}) collective-permute-start(bf16[2,256,4,128]{3,1,2,0:T(8,128)(2,1)S(1)} %get-tuple-element.447), channel_id=1, source_target_pairs={{0,4},{4,8},{8,12},{12,16},{16,20},{20,24},{24,28},{28,32},{32,36}... | collective-permute-start | bytes 1572872 | tf_op jit(solution)/shard_map/while/body/eval_jaxpr/ppermute | solution.py:14
  333.7 15.3 %collective-permute-start = (bf16[2,256,4,128]{3,1,2,0:T(8,128)(2,1)S(1)}, bf16[2,256,4,128]{3,1,2,0:T(8,128)(2,1)S(1)}, u32[]{:S(2)}, u32[]{:S(2)}) collective-permute-start(bf16[2,256,4,128]{3,1,2,0:T(8,128)(2,1)S(1)} %get-tuple-element.447), channel_id=1, source_target_pairs={{0,4},{4,8},{8,12},{12,16},{16,20},{20,24},{24,28},{28,32},{32,36}... | collective-permute-start | bytes 1572872 | tf_op jit(solution)/shard_map/while/body/eval_jaxpr/ppermute | solution.py:14
  350.0 14.3 %collective-permute-start = (bf16[2,256,4,128]{3,1,2,0:T(8,128)(2,1)S(1)}, bf16[2,256,4,128]{3,1,2,0:T(8,128)(2,1)S(1)}, u32[]{:S(2)}, u32[]{:S(2)}) collective-permute-start(bf16[2,256,4,128]{3,1,2,0:T(8,128)(2,1)S(1)} %get-tuple-element.447), channel_id=1, source_target_pairs={{0,4},{4,8},{8,12},{12,16},{16,20},{20,24},{24,28},{28,32},{32,36}... | collective-permute-start | bytes 1572872 | tf_op jit(solution)/shard_map/while/body/eval_jaxpr/ppermute | solution.py:14
  365.3 13.3 %collective-permute-start = (bf16[2,256,4,128]{3,1,2,0:T(8,128)(2,1)S(1)}, bf16[2,256,4,128]{3,1,2,0:T(8,128)(2,1)S(1)}, u32[]{:S(2)}, u32[]{:S(2)}) collective-permute-start(bf16[2,256,4,128]{3,1,2,0:T(8,128)(2,1)S(1)} %get-tuple-element.447), channel_id=1, source_target_pairs={{0,4},{4,8},{8,12},{12,16},{16,20},{20,24},{24,28},{28,32},{32,36}... | collective-permute-start | bytes 1572872 | tf_op jit(solution)/shard_map/while/body/eval_jaxpr/ppermute | solution.py:14
  379.7 12.4 %collective-permute-start = (bf16[2,256,4,128]{3,1,2,0:T(8,128)(2,1)S(1)}, bf16[2,256,4,128]{3,1,2,0:T(8,128)(2,1)S(1)}, u32[]{:S(2)}, u32[]{:S(2)}) collective-permute-start(bf16[2,256,4,128]{3,1,2,0:T(8,128)(2,1)S(1)} %get-tuple-element.447), channel_id=1, source_target_pairs={{0,4},{4,8},{8,12},{12,16},{16,20},{20,24},{24,28},{28,32},{32,36}... | collective-permute-start | bytes 1572872 | tf_op jit(solution)/shard_map/while/body/eval_jaxpr/ppermute | solution.py:14
  393.2 11.7 %collective-permute-start = (bf16[2,256,4,128]{3,1,2,0:T(8,128)(2,1)S(1)}, bf16[2,256,4,128]{3,1,2,0:T(8,128)(2,1)S(1)}, u32[]{:S(2)}, u32[]{:S(2)}) collective-permute-start(bf16[2,256,4,128]{3,1,2,0:T(8,128)(2,1)S(1)} %get-tuple-element.447), channel_id=1, source_target_pairs={{0,4},{4,8},{8,12},{12,16},{16,20},{20,24},{24,28},{28,32},{32,36}... | collective-permute-start | bytes 1572872 | tf_op jit(solution)/shard_map/while/body/eval_jaxpr/ppermute | solution.py:14
  406.0 12.3 %collective-permute-start = (bf16[2,256,4,128]{3,1,2,0:T(8,128)(2,1)S(1)}, bf16[2,256,4,128]{3,1,2,0:T(8,128)(2,1)S(1)}, u32[]{:S(2)}, u32[]{:S(2)}) collective-permute-start(bf16[2,256,4,128]{3,1,2,0:T(8,128)(2,1)S(1)} %get-tuple-element.447), channel_id=1, source_target_pairs={{0,4},{4,8},{8,12},{12,16},{16,20},{20,24},{24,28},{28,32},{32,36}... | collective-permute-start | bytes 1572872 | tf_op jit(solution)/shard_map/while/body/eval_jaxpr/ppermute | solution.py:14
  419.3 12.3 %collective-permute-start = (bf16[2,256,4,128]{3,1,2,0:T(8,128)(2,1)S(1)}, bf16[2,256,4,128]{3,1,2,0:T(8,128)(2,1)S(1)}, u32[]{:S(2)}, u32[]{:S(2)}) collective-permute-start(bf16[2,256,4,128]{3,1,2,0:T(8,128)(2,1)S(1)} %get-tuple-element.447), channel_id=1, source_target_pairs={{0,4},{4,8},{8,12},{12,16},{16,20},{20,24},{24,28},{28,32},{32,36}... | collective-permute-start | bytes 1572872 | tf_op jit(solution)/shard_map/while/body/eval_jaxpr/ppermute | solution.py:14
  432.7 12.6 %collective-permute-start = (bf16[2,256,4,128]{3,1,2,0:T(8,128)(2,1)S(1)}, bf16[2,256,4,128]{3,1,2,0:T(8,128)(2,1)S(1)}, u32[]{:S(2)}, u32[]{:S(2)}) collective-permute-start(bf16[2,256,4,128]{3,1,2,0:T(8,128)(2,1)S(1)} %get-tuple-element.447), channel_id=1, source_target_pairs={{0,4},{4,8},{8,12},{12,16},{16,20},{20,24},{24,28},{28,32},{32,36}... | collective-permute-start | bytes 1572872 | tf_op jit(solution)/shard_map/while/body/eval_jaxpr/ppermute | solution.py:14
  446.4 14.0 %collective-permute-start = (bf16[2,256,4,128]{3,1,2,0:T(8,128)(2,1)S(1)}, bf16[2,256,4,128]{3,1,2,0:T(8,128)(2,1)S(1)}, u32[]{:S(2)}, u32[]{:S(2)}) collective-permute-start(bf16[2,256,4,128]{3,1,2,0:T(8,128)(2,1)S(1)} %get-tuple-element.447), channel_id=1, source_target_pairs={{0,4},{4,8},{8,12},{12,16},{16,20},{20,24},{24,28},{28,32},{32,36}... | collective-permute-start | bytes 1572872 | tf_op jit(solution)/shard_map/while/body/eval_jaxpr/ppermute | solution.py:14
  461.4 15.1 %collective-permute-start = (bf16[2,256,4,128]{3,1,2,0:T(8,128)(2,1)S(1)}, bf16[2,256,4,128]{3,1,2,0:T(8,128)(2,1)S(1)}, u32[]{:S(2)}, u32[]{:S(2)}) collective-permute-start(bf16[2,256,4,128]{3,1,2,0:T(8,128)(2,1)S(1)} %get-tuple-element.447), channel_id=1, source_target_pairs={{0,4},{4,8},{8,12},{12,16},{16,20},{20,24},{24,28},{28,32},{32,36}... | collective-permute-start | bytes 1572872 | tf_op jit(solution)/shard_map/while/body/eval_jaxpr/ppermute | solution.py:14
  477.6 16.2 %collective-permute-start = (bf16[2,256,4,128]{3,1,2,0:T(8,128)(2,1)S(1)}, bf16[2,256,4,128]{3,1,2,0:T(8,128)(2,1)S(1)}, u32[]{:S(2)}, u32[]{:S(2)}) collective-permute-start(bf16[2,256,4,128]{3,1,2,0:T(8,128)(2,1)S(1)} %get-tuple-element.447), channel_id=1, source_target_pairs={{0,4},{4,8},{8,12},{12,16},{16,20},{20,24},{24,28},{28,32},{32,36}... | collective-permute-start | bytes 1572872 | tf_op jit(solution)/shard_map/while/body/eval_jaxpr/ppermute | solution.py:14
  494.8 17.3 %collective-permute-start = (bf16[2,256,4,128]{3,1,2,0:T(8,128)(2,1)S(1)}, bf16[2,256,4,128]{3,1,2,0:T(8,128)(2,1)S(1)}, u32[]{:S(2)}, u32[]{:S(2)}) collective-permute-start(bf16[2,256,4,128]{3,1,2,0:T(8,128)(2,1)S(1)} %get-tuple-element.447), channel_id=1, source_target_pairs={{0,4},{4,8},{8,12},{12,16},{16,20},{20,24},{24,28},{28,32},{32,36}... | collective-permute-start | bytes 1572872 | tf_op jit(solution)/shard_map/while/body/eval_jaxpr/ppermute | solution.py:14
  513.1 18.0 %collective-permute-start = (bf16[2,256,4,128]{3,1,2,0:T(8,128)(2,1)S(1)}, bf16[2,256,4,128]{3,1,2,0:T(8,128)(2,1)S(1)}, u32[]{:S(2)}, u32[]{:S(2)}) collective-permute-start(bf16[2,256,4,128]{3,1,2,0:T(8,128)(2,1)S(1)} %get-tuple-element.447), channel_id=1, source_target_pairs={{0,4},{4,8},{8,12},{12,16},{16,20},{20,24},{24,28},{28,32},{32,36}... | collective-permute-start | bytes 1572872 | tf_op jit(solution)/shard_map/while/body/eval_jaxpr/ppermute | solution.py:14
  537.1 182.5 %all-gather.13.cloned.1.call-start = ((), (), s32[]{:S(2)}) async-start(), calls=%async_computation.8 | async-start | bytes 4325376 | tf_op jit(solution)/shard_map/all_gather | solution.py:127
  538.7 263.7 %all-gather.15.cloned.1.call-start = ((), (), s32[]{:S(2)}) async-start(), calls=%async_computation.9 | async-start | bytes 4325376 | tf_op jit(solution)/shard_map/all_gather | solution.py:128
  540.4 269.2 %all-to-all-start.2 = ((bf16[4,1024,512]{2,1,0:T(8,128)(2,1)}), bf16[4,1024,512]{2,1,0:T(8,128)(2,1)}, u32[]{:S(2)}, u32[]{:S(2)}) async-start(bf16[4,1024,512]{2,1,0:T(8,128)(2,1)} %bitcast.83), calls=%async_computation.2 | async-start | bytes 8388608 | tf_op jit(solution)/shard_map/all_to_all | solution.py:134
  560.1 281.0 %reduce-scatter.2.cloned.1.call-start = ((), (), s32[]{:S(2)}) async-start(), calls=%async_computation.11 | async-start | bytes 1310720 | tf_op jit(solution)/shard_map/reduce_scatter | solution.py:135
Sparse Core Ops, SparseCore 0:
  10.5 89.1 all-gather.6
  102.8 68.9 all-gather.8
  174.9 68.9 all-gather.10
  246.8 91.9 all-gather.16
  537.2 89.9 all-reduce.1
  630.6 88.8 all-gather.12
  723.0 79.3 all-gather.14
  821.1 19.9 reduce-scatter.1
